TPU v7x, 512 devices: a whole 4x4x16 slice. The times are simulated.
512 devices in a mesh: rows: 64 (over x_hi, z, core), chan: 8 (over x_lo, y).
Axes of the slice: x: 4 (x_hi: 2, x_lo: 2; x = x_hi * 2 + x_lo), y: 4, z: 16, core: 2. Of those that a mesh axis runs over, the one named last changes fastest.
Arguments:
- hidden: float32 [32, 2048, 2048], P('chan', 'rows'), may hold values from -6 to 6
- front: float32 [2048, 2048], P('rows', 'chan'), may hold values from -6 to 6
- spectral_weight: float32 [2, 128, 128, 32, 32], P(None, 'rows', 'chan'), may hold values from -0.5 to 0.5
- skip_gain: float32 [32], P('chan'), may hold values from 0.5 to 1.5
- skip_bias: float32 [32], P('chan'), may hold values from -3 to 3
- project_weight: float32 [2, 32], P(None, 'chan'), may hold values from -1 to 1
- project_bias: float32 [2], replicated, may hold values from -3 to 3
- ice_mask: int32 [2048, 2048], P('rows', 'chan'), may hold values 0 or 1
- front_flags: int32 [2048, 2048], P('rows', 'chan'), may hold values 0 or 1
Outputs:
- velocity: float32 [2, 2048, 2048], P(None, 'rows', 'chan')
- front_next: float32 [2048, 2048], P('rows', 'chan')
All inputs are finite; a program needn't handle non-finite values. No bound on the sum of `ice_mask` or of `front_flags` on one device may be relied on, other than what follows from the above.
Results may differ from a plain program's by a relative error of at most 0.0003.
Values sent between devices are 32-bit elements; how exact they have to be, the bound alone decides.
No kernel may reach another device: no remote copies, remote signals or barrier semaphores. Data moves between devices by JAX's collectives and lax.ppermute only.
A program may use at most 128 MiB of HBM per device.

v0:
```python
import math
import jax
import jax.numpy as jnp
from jax import lax
from jax.sharding import PartitionSpec as P

LS_STEPS = 4
time_step = 0.25
highest = lax.Precision.HIGHEST


def with_halo(block, sides, width):
    for axis, dim in sides:
        count = lax.axis_size(axis)
        forward = [(i, i + 1) for i in range(count - 1)]
        backward = [(target, source) for source, target in forward]
        low = lax.ppermute(
            lax.slice_in_dim(block, block.shape[dim] - width, None, axis=dim), axis, forward
        )
        high = lax.ppermute(lax.slice_in_dim(block, 0, width, axis=dim), axis, backward)
        block = jnp.concatenate([low, block, high], axis=dim)
    return block


def angles(freqs, places, length):
    product = freqs[:, None] * places[None, :] % length
    return 2.0 * math.pi / length * product.astype(jnp.float32)


def x_tables(total_modes, places, length):
    mode_ids = jnp.arange(total_modes, dtype=jnp.int32)
    wave_ids = mode_ids - total_modes * (mode_ids >= total_modes // 2).astype(jnp.int32)
    phase = angles(wave_ids, places, length)
    return jnp.stack([jnp.cos(phase), jnp.sin(phase)])


def forward_x(spectra, tables):
    parts = jnp.einsum("cqrx,spx->cqrsp", spectra, tables, precision=highest)
    real_part = parts[:, :, 0, 0] + parts[:, :, 1, 1]
    imag_part = parts[:, :, 1, 0] - parts[:, :, 0, 1]
    return jnp.stack([real_part, imag_part], axis=2)


def inverse_x(spectra, tables):
    parts = jnp.einsum("cqrp,spx->cqrsx", spectra, tables, precision=highest)
    real_part = parts[:, :, 0, 0] - parts[:, :, 1, 1]
    imag_part = parts[:, :, 0, 1] + parts[:, :, 1, 0]
    stacked = jnp.stack([real_part, imag_part], axis=2)
    return stacked.reshape(stacked.shape[0], stacked.shape[1] * 2, stacked.shape[3])


def advance(padded, speed_x, speed_y, band):
    center = padded[1:-1, 1:-1]
    back_x = center - padded[:-2, 1:-1]
    ahead_x = padded[2:, 1:-1] - center
    back_y = center - padded[1:-1, :-2]
    ahead_y = padded[1:-1, 2:] - center
    transport = jnp.maximum(speed_x, 0.0) * back_x + jnp.minimum(speed_x, 0.0) * ahead_x
    transport = transport + jnp.maximum(speed_y, 0.0) * back_y + jnp.minimum(speed_y, 0.0) * ahead_y
    return center - time_step * band * transport


def on_device(
    hidden,
    front,
    spectral_weight,
    skip_gain,
    skip_bias,
    project_weight,
    project_bias,
    ice_mask,
    front_flags,
):
    local_chan, row_count, columns = hidden.shape
    row_devices = lax.axis_size("rows")
    chan_devices = lax.axis_size("chan")
    local_ymodes = spectral_weight.shape[1]
    all_rows = row_count * row_devices
    all_xmodes = spectral_weight.shape[2] * chan_devices
    all_ymodes = local_ymodes * row_devices
    norm_scale = 1.0 / math.sqrt(all_rows * columns * all_xmodes * all_ymodes)
    y_ids = jnp.arange(all_ymodes, dtype=jnp.int32)
    y_phase = angles(y_ids, jnp.arange(columns, dtype=jnp.int32), columns)
    forward_y = jnp.stack([jnp.cos(y_phase), -jnp.sin(y_phase)], axis=1).reshape(
        2 * all_ymodes, columns
    )
    y_weights = jnp.where(y_ids == 0, 1.0, 2.0).astype(jnp.float32)[:, None] * norm_scale
    inverse_y = jnp.stack(
        [y_weights * jnp.cos(y_phase), -y_weights * jnp.sin(y_phase)], axis=1
    ).reshape(2 * all_ymodes, columns)
    spec_y = jnp.einsum("cxy,ky->ckx", hidden, forward_y, precision=highest)
    own_rows = lax.axis_index("rows") * row_count + jnp.arange(row_count, dtype=jnp.int32)
    local_tables = x_tables(all_xmodes, own_rows, all_rows)
    picked = spec_y
    picked = picked.reshape(local_chan, local_ymodes * lax.axis_size("rows"), 2, row_count)
    owned = lax.psum_scatter(
        jnp.transpose(forward_x(picked, local_tables), (1, 0, 2, 3)),
        "rows",
        scatter_dimension=0,
        tiled=True,
    )
    spectra = jnp.transpose(owned, (1, 0, 2, 3))
    gathered = lax.all_to_all(spectra, "chan", split_axis=3, concat_axis=0, tiled=True)
    real_in = gathered[:, :, 0]
    imag_in = gathered[:, :, 1]
    real_out = jnp.einsum(
        "qpio,iqp->oqp", spectral_weight[0], real_in, precision=highest
    ) - jnp.einsum("qpio,iqp->oqp", spectral_weight[1], imag_in, precision=highest)
    imag_out = jnp.einsum(
        "qpio,iqp->oqp", spectral_weight[0], imag_in, precision=highest
    ) + jnp.einsum("qpio,iqp->oqp", spectral_weight[1], real_in, precision=highest)
    mixed = lax.all_to_all(
        jnp.stack([real_out, imag_out], axis=2), "chan", split_axis=0, concat_axis=3, tiled=True
    )
    inverted = inverse_x(lax.all_gather(mixed, "rows", axis=1, tiled=True), local_tables)
    spectral = jnp.einsum("ckx,ky->cxy", inverted, inverse_y, precision=highest)
    activated = jax.nn.gelu(
        spectral + skip_gain[:, None, None] * hidden + skip_bias[:, None, None], approximate=False
    )
    partial_speed = jnp.einsum("jc,cxy->jxy", project_weight, activated, precision=highest)
    tile_speed = (
        lax.psum_scatter(partial_speed, "chan", scatter_dimension=2, tiled=True)
        + project_bias[:, None, None]
    )
    velocity = tile_speed * ice_mask.astype(jnp.float32)[None]
    band = front_flags.astype(jnp.float32)
    level = front
    for level_step in range(LS_STEPS):
        padded = with_halo(level, (("rows", 0), ("chan", 1)), 1)
        level = advance(padded, velocity[0], velocity[1], band)
    return (velocity, level)


def solution(mesh):
    return jax.shard_map(
        on_device,
        mesh=mesh,
        in_specs=(
            P("chan", "rows", None),
            P("rows", "chan"),
            P(None, "rows", "chan", None, None),
            P("chan"),
            P("chan"),
            P(None, "chan"),
            P(),
            P("rows", "chan"),
            P("rows", "chan"),
        ),
        out_specs=(P(None, "rows", "chan"), P("rows", "chan")),
        check_vma=False,
    )
```

profile of v0, /device:TPU:28, one launch (start us, length us, event | category | flops | bytes accessed | tf_op | source)
XLA Modules:
  0.0 833.2 jit_solution(7316440260785637963)
XLA Ops:
  7.2 4.1 fusion.29
  11.6 1.6 copy.74
  13.2 2.4 reshape.371
  15.7 3.8 convolution_bitcast_fusion.2
  19.8 1.0 fusion.26
  20.9 1.1 copy.79
  22.1 1.3 dynamic-slice
  24.0 527.4 %all-reduce.3.cloned.1.call-done = f32[128,4,2,128]{3,1,2,0:T(4,128)} async-done(((f32[128,4,2,128]{3,1,2,0:T(4,128)}), f32[128,4,2,128]{3,1,2,0:T(4,128)}) %all-reduce.3.cloned.1.call-update) | async-done | bytes 524304
  551.4 0.7 dynamic-slice_bitcast_fusion
  552.4 0.9 reshape.391
  553.3 5.4 all-to-all-start
  558.7 4.1 all-to-all-done
  565.9 0.7 reshape.393
  566.6 5.3 all-to-all-start.1
  572.0 4.2 broadcast_multiply_fusion
  577.2 76.0 %all_gather.3 = f32[4,128,2,128]{3,0,2,1:T(4,128)S(1)} all-gather(f32[4,2,2,128]{3,0,2,1:T(4,128)S(1)} %reshape.387), channel_id=1, replica_groups=mesh['rows'=64,'chan'=8] {'rows'}, dimensions={1}, use_global_device_ids=true | all-gather | bytes 532480 | tf_op jit(solution)/shard_map/all_gather | solution.py:115
  653.2 0.7 fusion.20
  654.0 3.5 fusion.8
  657.5 2.5 convolution_bitcast_fusion.1
  660.0 26.2 %copy.126 = f32[2,32,2048]{0,1,2:T(8,128)} copy(f32[2,32,2048]{2,0,1:T(2,128)S(1)} %convolution_bitcast_fusion.1) | data formatting | bytes 1048576
  686.2 28.6 %reshape.388 = f32[2048,64]{1,0:T(8,128)} reshape(f32[2048,32,2]{2,1,0:T(8,128)} %bitcast.135) | data formatting | bytes 1048576
  714.8 2.3 collective-permute-start
  717.0 6.9 collective-permute-start.1
  724.0 1.2 collective-permute-done.1
  725.3 4.4 collective-permute-start.2
  729.8 2.1 collective-permute-start.3
  731.9 19.4 %reduce-scatter.4.cloned.1.call-done = f32[256,64]{1,0:T(8,128)} async-done(((f32[2048,64]{1,0:T(8,128)}), f32[256,64]{1,0:T(8,128)}) %reduce-scatter.4.cloned.1.call-update) | async-done | bytes 65552
  751.4 6.5 reshape.389
  757.8 3.6 copy.127
  761.8 1.9 collective-permute-start.4
  763.7 7.3 collective-permute-start.5
  771.0 1.3 collective-permute-done.5
  772.3 4.8 collective-permute-start.6
  777.2 1.9 collective-permute-start.7
  779.1 5.8 collective-permute-done.7
  785.1 1.9 collective-permute-start.8
  787.0 7.3 collective-permute-start.9
  794.3 1.3 collective-permute-done.9
  795.6 1.9 collective-permute-start.10
  797.5 3.9 collective-permute-start.11
  801.5 3.8 collective-permute-done.11
  805.4 1.9 collective-permute-start.12
  807.4 7.3 collective-permute-start.13
  814.6 1.3 collective-permute-done.13
  816.0 1.9 collective-permute-start.14
  817.9 3.9 collective-permute-start.15
  821.8 3.8 collective-permute-done.15
  825.7 0.7 fusion.44
  (86 shorter events, 5.8 us)
Async XLA Ops:
  7.2 650.3 %copy-start = (f32[2,4]{1,0:T(2,128)S(1)}, f32[2,4]{1,0:T(2,128)}, u32[]{:S(2)}) copy-start(f32[2,4]{1,0:T(2,128)} %param.14) | copy-start | bytes 100
  7.2 544.3 %all-reduce.3.cloned.1.call-start = ((), (), s32[]{:S(2)}) async-start(), calls=%async_computation.4 | async-start | bytes 1048576
  13.2 2.5 copy-start.1
  20.9 544.0 %copy-start.2 = (f32[2,2,16,32,32]{4,3,2,1,0:T(8,128)S(1)}, f32[2,2,16,32,32]{4,3,2,1,0:T(8,128)}, u32[]{:S(2)}) copy-start(f32[2,2,16,32,32]{4,3,2,1,0:T(8,128)} %param.11) | copy-start | bytes 786436
  553.3 9.5 %all-to-all-start = ((f32[8,1,256]{2,1,0:T(1,128)}), f32[8,1,256]{2,1,0:T(1,128)S(1)}, u32[]{:S(2)}, u32[]{:S(2)}) async-start(f32[8,1,256]{2,1,0:T(1,128)} %reshape.391), calls=%async_computation | async-start | bytes 16384 | tf_op jit(solution)/shard_map/all_to_all | solution.py:103
  566.6 9.6 %all-to-all-start.1 = ((f32[8,1,256]{2,1,0:T(1,128)}), f32[8,1,256]{2,1,0:T(1,128)S(1)}, u32[]{:S(2)}, u32[]{:S(2)}) async-start(f32[8,1,256]{2,1,0:T(1,128)} %reshape.393), calls=%async_computation.1 | async-start | bytes 16384 | tf_op jit(solution)/shard_map/all_to_all | solution.py:112
  572.0 82.0 %copy-start.8 = (f32[4]{0:T(128)S(1)}, f32[4]{0:T(128)}, u32[]{:S(2)}) copy-start(f32[4]{0:T(128)} %param.13) | copy-start | bytes 52
  572.0 82.0 %copy-start.9 = (f32[4]{0:T(128)S(1)}, f32[4]{0:T(128)}, u32[]{:S(2)}) copy-start(f32[4]{0:T(128)} %param.12) | copy-start | bytes 52
  572.0 179.4 %reduce-scatter.4.cloned.1.call-start = ((), (), s32[]{:S(2)}) async-start(), calls=%async_computation.3 | async-start | bytes 1179648
  686.2 28.6 %copy-start.5 = (f32[32,256]{1,0:T(8,128)S(1)}, f32[32,256]{1,0:T(8,128)}, u32[]{:S(2)}) copy-start(f32[32,256]{1,0:T(8,128)} %param.10) | copy-start | bytes 98308
  686.2 37.8 %copy-start.6 = (s32[32,256]{1,0:T(8,128)S(1)}, s32[32,256]{1,0:T(8,128)}, u32[]{:S(2)}) copy-start(s32[32,256]{1,0:T(8,128)} %param.16) | copy-start | bytes 98308
  714.8 9.2 %collective-permute-start = (f32[1,256]{1,0:T(1,128)S(1)}, f32[1,256]{1,0:T(1,128)S(1)}, u32[]{:S(2)}, u32[]{:S(2)}) collective-permute-start(f32[1,256]{1,0:T(1,128)S(1)} %get-tuple-element.36), channel_id=1, source_target_pairs={{0,8},{8,16},{16,24},{24,32},{32,40},{40,48},{48,56},{56,64},{64,7... | collective-permute-start | bytes 3080 | tf_op jit(solution)/shard_map/ppermute | solution.py:17
  717.0 8.2 collective-permute-start.1
  725.3 36.3 %collective-permute-start.2 = (f32[34,1]{1,0:T(8,128)S(1)}, f32[34,1]{1,0:T(8,128)S(1)}, u32[]{:S(2)}, u32[]{:S(2)}) collective-permute-start(f32[34,1]{1,0:T(8,128)S(1)} %get-tuple-element.28), channel_id=1, source_target_pairs={{0,1},{1,2},{2,3},{3,4},{4,5},{5,6},{6,7},{8,9},{9,10},{10,11},{11... | collective-permute-start | bytes 416 | tf_op jit(solution)/shard_map/ppermute | solution.py:17
  729.8 31.9 %collective-permute-start.3 = (f32[34,1]{1,0:T(8,128)S(1)}, f32[34,1]{1,0:T(8,128)S(1)}, u32[]{:S(2)}, u32[]{:S(2)}) collective-permute-start(f32[34,1]{1,0:T(8,128)S(1)} %get-tuple-element.29), channel_id=1, source_target_pairs={{1,0},{2,1},{3,2},{4,3},{5,4},{6,5},{7,6},{9,8},{10,9},{11,10},{12... | collective-permute-start | bytes 416 | tf_op jit(solution)/shard_map/ppermute | solution.py:20
  757.8 3.6 copy-start.7
  757.8 3.8 copy-start.4
  761.6 64.8 %copy-start.3 = (f32[2,32,256]{2,1,0:T(8,128)}, f32[2,32,256]{2,1,0:T(8,128)S(1)}, u32[]{:S(2)}) copy-start(f32[2,32,256]{2,1,0:T(8,128)S(1)} %copy.92) | copy-start | bytes 196612
  761.8 9.2 %collective-permute-start.4 = (f32[1,256]{1,0:T(1,128)S(1)}, f32[1,256]{1,0:T(1,128)S(1)}, u32[]{:S(2)}, u32[]{:S(2)}) collective-permute-start(f32[1,256]{1,0:T(1,128)S(1)} %get-tuple-element.34), channel_id=1, source_target_pairs={{0,8},{8,16},{16,24},{24,32},{32,40},{40,48},{48,56},{56,64},{64,7... | collective-permute-start | bytes 3080 | tf_op jit(solution)/shard_map/ppermute | solution.py:17
  763.7 8.5 %collective-permute-start.5 = (f32[1,256]{1,0:T(1,128)S(1)}, f32[1,256]{1,0:T(1,128)S(1)}, u32[]{:S(2)}, u32[]{:S(2)}) collective-permute-start(f32[1,256]{1,0:T(1,128)S(1)} %get-tuple-element.35), channel_id=1, source_target_pairs={{8,0},{16,8},{24,16},{32,24},{40,32},{48,40},{56,48},{64,56},{72,6... | collective-permute-start | bytes 3080 | tf_op jit(solution)/shard_map/ppermute | solution.py:20
  772.3 6.7 collective-permute-start.6
  777.2 7.8 collective-permute-start.7
  785.1 9.2 %collective-permute-start.8 = (f32[1,256]{1,0:T(1,128)S(1)}, f32[1,256]{1,0:T(1,128)S(1)}, u32[]{:S(2)}, u32[]{:S(2)}) collective-permute-start(f32[1,256]{1,0:T(1,128)S(1)} %get-tuple-element.32), channel_id=1, source_target_pairs={{0,8},{8,16},{16,24},{24,32},{32,40},{40,48},{48,56},{56,64},{64,7... | collective-permute-start | bytes 3080 | tf_op jit(solution)/shard_map/ppermute | solution.py:17
  787.0 8.5 %collective-permute-start.9 = (f32[1,256]{1,0:T(1,128)S(1)}, f32[1,256]{1,0:T(1,128)S(1)}, u32[]{:S(2)}, u32[]{:S(2)}) collective-permute-start(f32[1,256]{1,0:T(1,128)S(1)} %get-tuple-element.33), channel_id=1, source_target_pairs={{8,0},{16,8},{24,16},{32,24},{40,32},{48,40},{56,48},{64,56},{72,6... | collective-permute-start | bytes 3080 | tf_op jit(solution)/shard_map/ppermute | solution.py:20
  795.6 5.9 collective-permute-start.10
  797.5 7.8 collective-permute-start.11
  805.4 9.2 %collective-permute-start.12 = (f32[1,256]{1,0:T(1,128)S(1)}, f32[1,256]{1,0:T(1,128)S(1)}, u32[]{:S(2)}, u32[]{:S(2)}) collective-permute-start(f32[1,256]{1,0:T(1,128)S(1)} %get-tuple-element.30), channel_id=1, source_target_pairs={{0,8},{8,16},{16,24},{24,32},{32,40},{40,48},{48,56},{56,64},{64,7... | collective-permute-start | bytes 3080 | tf_op jit(solution)/shard_map/ppermute | solution.py:17
  807.4 8.5 %collective-permute-start.13 = (f32[1,256]{1,0:T(1,128)S(1)}, f32[1,256]{1,0:T(1,128)S(1)}, u32[]{:S(2)}, u32[]{:S(2)}) collective-permute-start(f32[1,256]{1,0:T(1,128)S(1)} %get-tuple-element.31), channel_id=1, source_target_pairs={{8,0},{16,8},{24,16},{32,24},{40,32},{48,40},{56,48},{64,56},{72,6... | collective-permute-start | bytes 3080 | tf_op jit(solution)/shard_map/ppermute | solution.py:20
  816.0 5.9 collective-permute-start.14
  817.9 7.8 collective-permute-start.15
Sparse Core Ops, SparseCore 0:
  22.2 529.1 all-reduce.2
  714.9 36.4 reduce-scatter.3
where the time goes:
time: 834 us; the launch traced here: 833 us
  waiting for transfers between devices  570 us (68%)
  local copies, waits for them, and re-layouts  76.4 us (9%)
  blocking collectives  76 us (9%)
  starting transfers between devices  72.4 us (9%)
  between operations  15.3 us (2%)
  other arithmetic  12 us (1%)
  matrix products  11.5 us (1%)
    unnamed x4, waiting for transfers between devices  547 us
    all_gather x1, blocking collectives, on_device(): lax.all_gather(mixed, 'rows', axis=1, tiled=True)  76 us
    unnamed x33, local copies, waits for them, and re-layouts  68.5 us
    ppermute x8, starting transfers between devices, with_halo(): lax.ppermute(lax.slice_in_dim(block, 0, width, axis=dim), axis, backward)  40.6 us
    ppermute x8, starting transfers between devices, with_halo(): lax.ppermute(lax.slice_in_dim(block, block.shape[dim] - width, None, axis...  21.1 us
    ppermute x8, waiting for transfers between devices, with_halo(): lax.ppermute(lax.slice_in_dim(block, 0, width, axis=dim), axis, backward)  18.6 us
  transfers between devices with their start and end apart: 20, of which 10 were waited for; matrix products, arithmetic and copies ran while one was open for 2% of the time, Pallas kernels for 0%

commit v1 on v0

--- a/solution.py
+++ b/solution.py
@@ -112,7 +112,12 @@
     mixed = lax.all_to_all(
         jnp.stack([real_out, imag_out], axis=2), "chan", split_axis=0, concat_axis=3, tiled=True
     )
-    inverted = inverse_x(lax.all_gather(mixed, "rows", axis=1, tiled=True), local_tables)
+    inverted = inverse_x(
+        jnp.concatenate(
+            lax.all_to_all(jnp.stack([mixed] * lax.axis_size("rows")), "rows", 0, 0), axis=1
+        ),
+        local_tables,
+    )
     spectral = jnp.einsum("ckx,ky->cxy", inverted, inverse_y, precision=highest)
     activated = jax.nn.gelu(
         spectral + skip_gain[:, None, None] * hidden + skip_bias[:, None, None], approximate=False

time: 834 us -> 799 us (0.958)
  blocking collectives: 76 us -> 17.9 us
  waiting for transfers between devices: 570 us -> 593 us
    all_gather x1 -> x0, blocking collectives: 76 us -> none  [on_device(): lax.all_gather(mixed, 'rows', axis=1, tiled=True)]
    all_to_all x2 -> x1, waiting for transfers between devices: 4.13 us -> 23.8 us  [on_device(): lax.all_to_all(jnp.stack([mixed] * lax.axis_size('rows')), 'rows', 0, 0)]
    all_to_all x0 -> x2, blocking collectives: none -> 17.9 us  [the longest x1 9.32 us: on_device(): lax.all_to_all(spectra, 'chan', split_axis=3, concat_axis=0, tiled=True)]
    unnamed x33 -> x37, local copies, waits for them, and re-layouts: 68.5 us -> 67.9 us
  transfers between devices with their start and end apart: 20 -> 19, of which waited for: 10 -> 10; matrix products, arithmetic and copies ran while one was open for 2% -> 2% of each run, Pallas kernels for 0% -> 0%
where the time goes in v1:
time: 799 us; the launch traced here: 798 us
  waiting for transfers between devices  593 us (74%)
  local copies, waits for them, and re-layouts  76.9 us (10%)
  starting transfers between devices  69.5 us (9%)
  blocking collectives  17.9 us (2%)
  between operations  15.3 us (2%)
  other arithmetic  13.4 us (2%)
  matrix products  11.4 us (1%)
    unnamed x4, waiting for transfers between devices  551 us
    unnamed x37, local copies, waits for them, and re-layouts  67.9 us
    ppermute x8, starting transfers between devices, with_halo(): lax.ppermute(lax.slice_in_dim(block, 0, width, axis=dim), axis, backward)  40.3 us
    all_to_all x1, waiting for transfers between devices, on_device(): lax.all_to_all(jnp.stack([mixed] * lax.axis_size('rows')), 'rows', 0, 0)  23.8 us
    ppermute x8, starting transfers between devices, with_halo(): lax.ppermute(lax.slice_in_dim(block, block.shape[dim] - width, None, axis...  21.2 us
    ppermute x8, waiting for transfers between devices, with_halo(): lax.ppermute(lax.slice_in_dim(block, 0, width, axis=dim), axis, backward)  18.6 us
  transfers between devices with their start and end apart: 19, of which 10 were waited for; matrix products, arithmetic and copies ran while one was open for 2% of the time, Pallas kernels for 0%

profile of v1, /device:TPU:28, one launch (start us, length us, event | category | flops | bytes accessed | tf_op | source)
XLA Modules:
  0.0 797.5 jit_solution(4239131399082929265)
XLA Ops:
  7.2 4.1 fusion.27
  11.6 1.6 copy.71
  13.2 2.4 reshape.382
  15.7 3.8 convolution_bitcast_fusion.2
  19.8 1.0 fusion.24
  20.9 1.1 copy.76
  22.1 1.3 dynamic-slice
  24.0 527.7 %all-reduce.3.cloned.1.call-done = f32[128,4,2,128]{3,1,2,0:T(4,128)} async-done(((f32[128,4,2,128]{3,1,2,0:T(4,128)}), f32[128,4,2,128]{3,1,2,0:T(4,128)}) %all-reduce.3.cloned.1.call-update) | async-done | bytes 524304
  551.7 0.7 dynamic-slice_bitcast_fusion
  553.0 9.3 %all_to_all.38 = f32[8,1,256]{2,1,0:T(1,128)S(1)} all-to-all(f32[8,1,256]{2,1,0:T(1,128)S(1)} %reshape.402), channel_id=1, replica_groups=mesh['rows'=64,'chan'=8] {'chan'}, dimensions={0} | all-to-all | bytes 16384 | tf_op jit(solution)/shard_map/all_to_all | solution.py:103
  565.5 8.6 %all_to_all.39 = f32[8,1,256]{2,1,0:T(1,128)S(1)} all-to-all(f32[8,1,256]{2,1,0:T(1,128)S(1)} %reshape.404), channel_id=1, replica_groups=mesh['rows'=64,'chan'=8] {'chan'}, dimensions={0} | all-to-all | bytes 16384 | tf_op jit(solution)/shard_map/all_to_all | solution.py:112
  574.1 0.7 reduce.9
  575.0 0.9 stack.27
  575.9 7.9 all-to-all-start.2
  584.0 5.6 broadcast_multiply_fusion
  589.5 23.8 %all-to-all-done.2 = f32[64,4,2,2,128]{4,2,3,1,0:T(2,128)S(1)} async-done(((f32[64,4,2,2,128]{4,2,3,1,0:T(2,128)}), f32[64,4,2,2,128]{4,2,3,1,0:T(2,128)S(1)}, u32[]{:S(2)}, u32[]{:S(2)}) %all-to-all-start.2) | async-done | bytes 524320 | tf_op jit(solution)/shard_map/all_to_all | solution.py:117
  613.6 0.7 fusion.90
  614.9 3.5 fusion.8
  618.4 2.5 convolution_bitcast_fusion.1
  620.9 26.2 %copy.121 = f32[2,32,2048]{0,1,2:T(8,128)} copy(f32[2,32,2048]{2,0,1:T(2,128)S(1)} %convolution_bitcast_fusion.1) | data formatting | bytes 1048576
  647.1 28.6 %reshape.399 = f32[2048,64]{1,0:T(8,128)} reshape(f32[2048,32,2]{2,1,0:T(8,128)} %bitcast.141) | data formatting | bytes 1048576
  675.7 2.6 collective-permute-start
  678.3 6.6 collective-permute-start.1
  684.9 1.2 collective-permute-done.1
  686.3 4.0 collective-permute-start.2
  690.3 2.1 collective-permute-start.3
  692.4 23.0 %reduce-scatter.4.cloned.1.call-done = f32[256,64]{1,0:T(8,128)} async-done(((f32[2048,64]{1,0:T(8,128)}), f32[256,64]{1,0:T(8,128)}) %reduce-scatter.4.cloned.1.call-update) | async-done | bytes 65552
  715.4 6.5 reshape.400
  721.9 3.6 copy.122
  725.8 1.9 collective-permute-start.4
  727.7 7.3 collective-permute-start.5
  735.0 1.3 collective-permute-done.5
  736.4 5.1 collective-permute-start.6
  741.4 1.9 collective-permute-start.7
  743.4 5.8 collective-permute-done.7
  749.3 1.9 collective-permute-start.8
  751.3 7.3 collective-permute-start.9
  758.6 1.3 collective-permute-done.9
  759.9 1.9 collective-permute-start.10
  761.8 3.9 collective-permute-start.11
  765.8 3.8 collective-permute-done.11
  769.7 1.9 collective-permute-start.12
  771.7 7.3 collective-permute-start.13
  778.9 1.3 collective-permute-done.13
  780.3 1.9 collective-permute-start.14
  782.2 3.9 collective-permute-start.15
  786.1 3.8 collective-permute-done.15
  790.0 0.7 fusion.42
  (91 shorter events, 6.4 us)
Async XLA Ops:
  7.2 611.2 %copy-start = (f32[2,4]{1,0:T(2,128)S(1)}, f32[2,4]{1,0:T(2,128)}, u32[]{:S(2)}) copy-start(f32[2,4]{1,0:T(2,128)} %param.14) | copy-start | bytes 100
  7.2 544.5 %all-reduce.3.cloned.1.call-start = ((), (), s32[]{:S(2)}) async-start(), calls=%async_computation.5 | async-start | bytes 1048576
  13.2 2.5 copy-start.1
  20.9 543.5 %copy-start.2 = (f32[2,2,16,32,32]{4,3,2,1,0:T(8,128)S(1)}, f32[2,2,16,32,32]{4,3,2,1,0:T(8,128)}, u32[]{:S(2)}) copy-start(f32[2,2,16,32,32]{4,3,2,1,0:T(8,128)} %param.11) | copy-start | bytes 786436
  575.9 37.4 %all-to-all-start.2 = ((f32[64,4,2,2,128]{4,2,3,1,0:T(2,128)}), f32[64,4,2,2,128]{4,2,3,1,0:T(2,128)S(1)}, u32[]{:S(2)}, u32[]{:S(2)}) async-start(f32[64,4,2,2,128]{4,2,3,1,0:T(2,128)} %stack.27), calls=%async_computation.2 | async-start | bytes 1048576 | tf_op jit(solution)/shard_map/all_to_all | solution.py:117
  583.9 131.5 %reduce-scatter.4.cloned.1.call-start = ((), (), s32[]{:S(2)}) async-start(), calls=%async_computation.4 | async-start | bytes 1179648
  583.9 30.4 %copy-start.10 = (f32[4]{0:T(128)S(1)}, f32[4]{0:T(128)}, u32[]{:S(2)}) copy-start(f32[4]{0:T(128)} %param.13) | copy-start | bytes 52
  583.9 30.4 %copy-start.11 = (f32[4]{0:T(128)S(1)}, f32[4]{0:T(128)}, u32[]{:S(2)}) copy-start(f32[4]{0:T(128)} %param.12) | copy-start | bytes 52
  613.4 1.2 copy-start.3
  613.4 1.5 copy-start.4
  647.1 28.6 %copy-start.7 = (f32[32,256]{1,0:T(8,128)S(1)}, f32[32,256]{1,0:T(8,128)}, u32[]{:S(2)}) copy-start(f32[32,256]{1,0:T(8,128)} %param.10) | copy-start | bytes 98308
  647.1 37.8 %copy-start.8 = (s32[32,256]{1,0:T(8,128)S(1)}, s32[32,256]{1,0:T(8,128)}, u32[]{:S(2)}) copy-start(s32[32,256]{1,0:T(8,128)} %param.16) | copy-start | bytes 98308
  675.7 9.2 %collective-permute-start = (f32[1,256]{1,0:T(1,128)S(1)}, f32[1,256]{1,0:T(1,128)S(1)}, u32[]{:S(2)}, u32[]{:S(2)}) collective-permute-start(f32[1,256]{1,0:T(1,128)S(1)} %get-tuple-element.36), channel_id=1, source_target_pairs={{0,8},{8,16},{16,24},{24,32},{32,40},{40,48},{48,56},{56,64},{64,7... | collective-permute-start | bytes 3080 | tf_op jit(solution)/shard_map/ppermute | solution.py:17
  678.3 7.9 collective-permute-start.1
  686.3 39.4 %collective-permute-start.2 = (f32[34,1]{1,0:T(8,128)S(1)}, f32[34,1]{1,0:T(8,128)S(1)}, u32[]{:S(2)}, u32[]{:S(2)}) collective-permute-start(f32[34,1]{1,0:T(8,128)S(1)} %get-tuple-element.28), channel_id=1, source_target_pairs={{0,1},{1,2},{2,3},{3,4},{4,5},{5,6},{6,7},{8,9},{9,10},{10,11},{11... | collective-permute-start | bytes 416 | tf_op jit(solution)/shard_map/ppermute | solution.py:17
  690.3 35.4 %collective-permute-start.3 = (f32[34,1]{1,0:T(8,128)S(1)}, f32[34,1]{1,0:T(8,128)S(1)}, u32[]{:S(2)}, u32[]{:S(2)}) collective-permute-start(f32[34,1]{1,0:T(8,128)S(1)} %get-tuple-element.29), channel_id=1, source_target_pairs={{1,0},{2,1},{3,2},{4,3},{5,4},{6,5},{7,6},{9,8},{10,9},{11,10},{12... | collective-permute-start | bytes 416 | tf_op jit(solution)/shard_map/ppermute | solution.py:20
  721.9 3.6 copy-start.9
  721.9 3.8 copy-start.6
  725.7 65.1 %copy-start.5 = (f32[2,32,256]{2,1,0:T(8,128)}, f32[2,32,256]{2,1,0:T(8,128)S(1)}, u32[]{:S(2)}) copy-start(f32[2,32,256]{2,1,0:T(8,128)S(1)} %copy.89) | copy-start | bytes 196612
  725.8 9.2 %collective-permute-start.4 = (f32[1,256]{1,0:T(1,128)S(1)}, f32[1,256]{1,0:T(1,128)S(1)}, u32[]{:S(2)}, u32[]{:S(2)}) collective-permute-start(f32[1,256]{1,0:T(1,128)S(1)} %get-tuple-element.34), channel_id=1, source_target_pairs={{0,8},{8,16},{16,24},{24,32},{32,40},{40,48},{48,56},{56,64},{64,7... | collective-permute-start | bytes 3080 | tf_op jit(solution)/shard_map/ppermute | solution.py:17
  727.7 8.5 %collective-permute-start.5 = (f32[1,256]{1,0:T(1,128)S(1)}, f32[1,256]{1,0:T(1,128)S(1)}, u32[]{:S(2)}, u32[]{:S(2)}) collective-permute-start(f32[1,256]{1,0:T(1,128)S(1)} %get-tuple-element.35), channel_id=1, source_target_pairs={{8,0},{16,8},{24,16},{32,24},{40,32},{48,40},{56,48},{64,56},{72,6... | collective-permute-start | bytes 3080 | tf_op jit(solution)/shard_map/ppermute | solution.py:20
  736.4 7.0 collective-permute-start.6
  741.4 7.8 collective-permute-start.7
  749.3 9.2 %collective-permute-start.8 = (f32[1,256]{1,0:T(1,128)S(1)}, f32[1,256]{1,0:T(1,128)S(1)}, u32[]{:S(2)}, u32[]{:S(2)}) collective-permute-start(f32[1,256]{1,0:T(1,128)S(1)} %get-tuple-element.32), channel_id=1, source_target_pairs={{0,8},{8,16},{16,24},{24,32},{32,40},{40,48},{48,56},{56,64},{64,7... | collective-permute-start | bytes 3080 | tf_op jit(solution)/shard_map/ppermute | solution.py:17
  751.3 8.5 %collective-permute-start.9 = (f32[1,256]{1,0:T(1,128)S(1)}, f32[1,256]{1,0:T(1,128)S(1)}, u32[]{:S(2)}, u32[]{:S(2)}) collective-permute-start(f32[1,256]{1,0:T(1,128)S(1)} %get-tuple-element.33), channel_id=1, source_target_pairs={{8,0},{16,8},{24,16},{32,24},{40,32},{48,40},{56,48},{64,56},{72,6... | collective-permute-start | bytes 3080 | tf_op jit(solution)/shard_map/ppermute | solution.py:20
  759.9 5.9 collective-permute-start.10
  761.8 7.8 collective-permute-start.11
  769.7 9.2 %collective-permute-start.12 = (f32[1,256]{1,0:T(1,128)S(1)}, f32[1,256]{1,0:T(1,128)S(1)}, u32[]{:S(2)}, u32[]{:S(2)}) collective-permute-start(f32[1,256]{1,0:T(1,128)S(1)} %get-tuple-element.30), channel_id=1, source_target_pairs={{0,8},{8,16},{16,24},{24,32},{32,40},{40,48},{48,56},{56,64},{64,7... | collective-permute-start | bytes 3080 | tf_op jit(solution)/shard_map/ppermute | solution.py:17
  771.7 8.5 %collective-permute-start.13 = (f32[1,256]{1,0:T(1,128)S(1)}, f32[1,256]{1,0:T(1,128)S(1)}, u32[]{:S(2)}, u32[]{:S(2)}) collective-permute-start(f32[1,256]{1,0:T(1,128)S(1)} %get-tuple-element.31), channel_id=1, source_target_pairs={{8,0},{16,8},{24,16},{32,24},{40,32},{48,40},{56,48},{64,56},{72,6... | collective-permute-start | bytes 3080 | tf_op jit(solution)/shard_map/ppermute | solution.py:20
  780.3 5.9 collective-permute-start.14
  782.2 7.8 collective-permute-start.15
Sparse Core Ops, SparseCore 0:
  22.2 529.4 all-reduce.2
  675.8 39.5 reduce-scatter.3
